TPU v7x, 256 devices: a whole 4x4x8 slice. The times are simulated.
256 devices in a mesh: group: 4 (over y), shard: 16 (over x_hi, z), tensor: 4 (over x_lo, core).
Axes of the slice: x: 4 (x_hi: 2, x_lo: 2; x = x_hi * 2 + x_lo), y: 4, z: 8, core: 2. Of those that a mesh axis runs over, the one named last changes fastest.
Arguments:
- group_weights: bfloat16 [4, 8, 1024, 8704], P('group', None, None, ('shard', 'tensor')), may hold values from -6 to 6
- anchor: float32 [8, 1024, 16, 4, 136], P(None, ('group', 'shard'), None, 'tensor'), may hold values from -6 to 6
- momentum: float32 [8, 1024, 16, 4, 136], P(None, ('group', 'shard'), None, 'tensor'), may hold values from -6 to 6
- group_embedding: bfloat16 [4, 32000, 1024], P('group', 'shard', 'tensor'), may hold values from -6 to 6
- emb_anchor: float32 [32000, 1024], P('shard', 'tensor'), may hold values from -6 to 6
- emb_momentum: float32 [32000, 1024], P('shard', 'tensor'), may hold values from -6 to 6
- basis: float32 [1024, 64], P('tensor'), may hold values from -0.1875 to 0.1875
Outputs:
- new_weights: bfloat16 [8, 1024, 8704], P(None, None, ('shard', 'tensor'))
- new_anchor: float32 [8, 1024, 16, 4, 136], P(None, ('group', 'shard'), None, 'tensor')
- new_momentum: float32 [8, 1024, 16, 4, 136], P(None, ('group', 'shard'), None, 'tensor')
- new_embedding: bfloat16 [32000, 1024], P('shard', 'tensor')
- new_emb_anchor: float32 [32000, 1024], P('shard', 'tensor')
- new_emb_momentum: float32 [32000, 1024], P('shard', 'tensor')
All inputs are finite; a program needn't handle non-finite values.
Results may differ from a plain program's by a relative error of at most 0.012.
Values may be sent and summed in bfloat16 or wider, within the bound.
No kernel may reach another device: no remote copies, remote signals or barrier semaphores. Data moves between devices by JAX's collectives and lax.ppermute only.
A program may use at most 128 MiB of HBM per device.

v0:
```python
import jax
import jax.numpy as jnp
from jax import lax
from jax.sharding import PartitionSpec as P

outer_rate = 0.7
momentum_decay = 0.9


def per_device(group_weights, anchor, momentum, group_embedding, emb_anchor, emb_momentum, basis):
    groups = lax.axis_size("group")
    layers = group_weights.shape[1]
    width = group_weights.shape[2]
    block = group_weights.shape[3]
    local_weights = group_weights[0]
    part = lax.psum_scatter(
        local_weights.astype(jnp.float32).astype(jnp.bfloat16),
        "group",
        scatter_dimension=1,
        tiled=True,
    ).astype(jnp.float32)
    part = part.reshape(layers, part.shape[1], 1, 1, block)
    summed = lax.all_to_all(part, "shard", split_axis=1, concat_axis=2, tiled=True)
    delta = anchor - summed / groups
    moved = momentum_decay * momentum + delta
    stepped = anchor - outer_rate * (delta + momentum_decay * moved)
    stepped_half = stepped.astype(jnp.bfloat16)
    columns = lax.all_to_all(stepped_half, "shard", split_axis=2, concat_axis=1, tiled=True)
    whole = lax.all_gather(columns, "group", axis=1, tiled=True)
    new_weights = whole.reshape(layers, width, block)
    local_embedding = group_embedding[0].astype(jnp.float32)
    emb_sum = lax.psum(local_embedding.astype(jnp.bfloat16), "group").astype(jnp.float32)
    difference = emb_anchor - emb_sum / groups
    coef = lax.psum(jnp.dot(difference, basis, precision=lax.Precision.HIGHEST), "tensor")
    emb_delta = jnp.dot(coef, basis.T, precision=lax.Precision.HIGHEST)
    emb_moved = momentum_decay * emb_momentum + emb_delta
    emb_stepped = emb_anchor - outer_rate * (emb_delta + momentum_decay * emb_moved)
    return (new_weights, stepped, moved, emb_stepped.astype(jnp.bfloat16), emb_stepped, emb_moved)


def solution(mesh):
    return jax.shard_map(
        per_device,
        mesh=mesh,
        in_specs=(
            P("group", None, None, ("shard", "tensor")),
            P(None, ("group", "shard"), None, "tensor", None),
            P(None, ("group", "shard"), None, "tensor", None),
            P("group", "shard", "tensor"),
            P("shard", "tensor"),
            P("shard", "tensor"),
            P("tensor", None),
        ),
        out_specs=(
            P(None, None, ("shard", "tensor")),
            P(None, ("group", "shard"), None, "tensor", None),
            P(None, ("group", "shard"), None, "tensor", None),
            P("shard", "tensor"),
            P("shard", "tensor"),
            P("shard", "tensor"),
        ),
        check_vma=False,
    )
```

profile of v0, /device:TPU:1, one launch (start us, length us, event | category | flops | bytes accessed | tf_op | source)
XLA Modules:
  0.0 260.1 jit_solution(16609563485341192564)
XLA Ops:
  7.2 0.0 copy-start
  7.2 0.0 reduce-scatter.2.cloned.1.call-start
  7.2 6.8 %copy.20 = bf16[1,8,1024,136]{3,1,2,0:T(8,128)(2,1)} copy(bf16[1,8,1024,136]{2,3,1,0:T(8,128)(2,1)} %param.7) | data formatting | bytes 4456448 | tf_op args[0]
  14.0 0.0 reduce-scatter.2.cloned.1.call-update
  14.0 53.3 %reduce-scatter.2.cloned.1.call-done = bf16[8,256,136]{2,0,1:T(8,128)(2,1)} async-done(((bf16[8,1024,136]{2,0,1:T(8,128)(2,1)}), bf16[8,256,136]{2,0,1:T(8,128)(2,1)}) %reduce-scatter.2.cloned.1.call-update) | async-done | bytes 557072 | tf_op jit(solution)/shard_map/reduce_scatter | solution.py:16
  67.3 2.7 %bitcast_convert_fusion = f32[8,256,1,1,136]{4,0,3,2,1:T(8,128)} fusion(bf16[8,256,136]{2,0,1:T(8,128)(2,1)} %reduce-scatter.2.cloned.1.call-done), kind=kLoop, calls=%fused_computation.11 | loop fusion | flops 278528 | bytes 1671168 | tf_op jit(solution)/shard_map/reshape | solution.py:22
  70.0 9.2 %all-to-all-start = ((f32[8,256,1,1,136]{4,0,3,2,1:T(8,128)}), f32[8,256,1,1,136]{4,0,3,2,1:T(8,128)S(1)}, u32[]{:S(2)}, u32[]{:S(2)}) async-start(f32[8,256,1,1,136]{4,0,3,2,1:T(8,128)} %bitcast_convert_fusion), calls=%async_computation.1 | async-start | bytes 4194304 | tf_op jit(solution)/shard_map/all_to_all | solution.py:23
  79.3 0.0 all-reduce.3.cloned.1.call-start
  79.3 0.7 all-reduce.3.cloned.1.call-update
  80.0 48.4 %all-to-all-done = f32[8,256,1,1,136]{4,0,3,2,1:T(8,128)S(1)} async-done(((f32[8,256,1,1,136]{4,0,3,2,1:T(8,128)}), f32[8,256,1,1,136]{4,0,3,2,1:T(8,128)S(1)}, u32[]{:S(2)}, u32[]{:S(2)}) %all-to-all-start) | async-done | bytes 1114144 | tf_op jit(solution)/shard_map/all_to_all | solution.py:23
  128.5 0.7 copy_multiply_fusion.1
  129.2 0.9 copy-done.2
  130.1 0.6 copy-done.3
  130.7 5.1 %fusion.8 = (bf16[8,16,16,1,136]{4,1,2,0,3:T(8,128)(2,1)S(1)}, f32[8,16,16,1,136]{4,1,2,0,3:T(8,128)}, f32[8,16,16,1,136]{4,1,2,0,3:T(8,128)S(1)}) fusion(f32[8,16,16,1,136]{4,3,2,1,0:T(1,128)S(1)} %copy-done.2, f32[8,16,16,1,136]{4,1,2,0,3:T(8,128)S(1)} %bitcast.19, f32[8,16,16,1,136]{4,3,2,1,0:T(1,128)S(1)} %copy-done.3), kind=kLoop, calls=%fused_computation.15 | loop fusion | flops 2228224 | bytes 6127616 | tf_op jit(solution)/shard_map/convert_element_type | solution.py:27
  135.8 1.1 copy.25
  136.9 7.1 %all-to-all-start.1 = ((bf16[8,16,16,1,136]{4,1,0,3,2:T(8,128)(2,1)}), bf16[8,16,16,1,136]{4,1,0,3,2:T(8,128)(2,1)S(1)}, u32[]{:S(2)}, u32[]{:S(2)}) async-start(bf16[8,16,16,1,136]{4,1,0,3,2:T(8,128)(2,1)} %copy.25), calls=%async_computation.2 | async-start | bytes 2097152 | tf_op jit(solution)/shard_map/all_to_all | solution.py:28
  144.0 0.0 all-reduce.5.cloned.1.call-start
  144.1 0.0 all-reduce.3.cloned.1.call-done
  144.1 0.0 copy-done
  144.1 4.8 %fusion.1 = f32[2000,64]{0,1:T(8,128)} fusion(f32[256,64]{0,1:T(8,128)S(1)} %copy-done, f32[2000,256]{1,0:T(8,128)} %param.11, bf16[2000,256]{1,0:T(8,128)(2,1)} %all-reduce.3.cloned.1.call-done), kind=kOutput, calls=%fused_computation.6 | convolution fusion | flops 394752000 | bytes 3649536 | tf_op jit(solution)/shard_map/dot_general | solution.py:34
  148.9 0.0 all-reduce.5.cloned.1.call-update
  148.9 0.2 all-gather.2.cloned.1.call-start
  149.1 21.9 %all-to-all-done.1 = bf16[8,16,16,1,136]{4,1,0,3,2:T(8,128)(2,1)S(1)} async-done(((bf16[8,16,16,1,136]{4,1,0,3,2:T(8,128)(2,1)}), bf16[8,16,16,1,136]{4,1,0,3,2:T(8,128)(2,1)S(1)}, u32[]{:S(2)}, u32[]{:S(2)}) %all-to-all-start.1) | async-done | bytes 557088 | tf_op jit(solution)/shard_map/all_to_all | solution.py:28
  171.1 1.1 copy.26
  172.2 0.0 all-gather.2.cloned.1.call-update
  172.2 22.1 %all-reduce.5.cloned.1.call-done = f32[2000,64]{0,1:T(8,128)} async-done(((f32[2000,64]{0,1:T(8,128)}), f32[2000,64]{0,1:T(8,128)}) %all-reduce.5.cloned.1.call-update) | async-done | bytes 512016 | tf_op jit(solution)/shard_map/psum | solution.py:34
  194.3 6.9 %fusion.7 = (bf16[2000,256]{1,0:T(8,128)(2,1)}, f32[2000,256]{1,0:T(8,128)}, f32[2000,256]{1,0:T(8,128)}) fusion(f32[2000,256]{1,0:T(8,128)} %param.11, f32[2000,256]{1,0:T(8,128)} %param.12, f32[2000,64]{0,1:T(8,128)} %all-reduce.5.cloned.1.call-done, f32[256,64]{0,1:T(8,128)S(1)} %copy-done), kind=kOutput, calls=%fused_computation.14 | convolution fusion | flops 396800000 | bytes 9793536 | tf_op jit(solution)/shard_map/dot_general | solution.py:35
  201.3 0.0 copy-done.1
  201.3 3.7 %copy.28 = f32[8,16,16,1,136]{4,3,2,1,0:T(1,128)} copy(f32[8,16,16,1,136]{4,1,2,0,3:T(8,128)S(1)} %copy-done.1) | data formatting | bytes 2228224
  205.0 3.7 %copy.29 = f32[8,16,16,1,136]{4,3,2,1,0:T(1,128)} copy(f32[8,16,16,1,136]{4,1,2,0,3:T(8,128)S(1)} %get-tuple-element.23) | data formatting | bytes 2228224
  208.7 39.0 %all-gather.2.cloned.1.call-done = bf16[8,1024,1,1,136]{4,1,0,3,2:T(8,128)(2,1)} async-done(((bf16[8,256,1,1,136]{4,1,0,3,2:T(8,128)(2,1)}), bf16[8,1024,1,1,136]{4,1,0,3,2:T(8,128)(2,1)}) %all-gather.2.cloned.1.call-update) | async-done | bytes 2228240 | tf_op jit(solution)/shard_map/all_gather | solution.py:29
  247.7 5.9 %copy.27 = bf16[8,1024,136]{1,2,0:T(8,128)(2,1)} copy(bf16[8,1024,136]{2,1,0:T(8,128)(2,1)} %bitcast.20) | data formatting | bytes 4456448
  (3 shorter events, 0.0 us)
Async XLA Ops:
  7.2 136.9 %copy-start = (f32[256,64]{0,1:T(8,128)S(1)}, f32[256,64]{0,1:T(8,128)}, u32[]{:S(2)}) copy-start(f32[256,64]{0,1:T(8,128)} %param.13) | copy-start | bytes 196612
  7.2 60.1 %reduce-scatter.2.cloned.1.call-start = ((), (), s32[]{:S(2)}) async-start(), calls=%async_computation.3 | async-start | bytes 5242880 | tf_op jit(solution)/shard_map/reduce_scatter | solution.py:16
  70.0 58.4 %all-to-all-start = ((f32[8,256,1,1,136]{4,0,3,2,1:T(8,128)}), f32[8,256,1,1,136]{4,0,3,2,1:T(8,128)S(1)}, u32[]{:S(2)}, u32[]{:S(2)}) async-start(f32[8,256,1,1,136]{4,0,3,2,1:T(8,128)} %bitcast_convert_fusion), calls=%async_computation.1 | async-start | bytes 4194304 | tf_op jit(solution)/shard_map/all_to_all | solution.py:23
  79.3 64.8 %all-reduce.3.cloned.1.call-start = ((), (), s32[]{:S(2)}) async-start(), calls=%async_computation.5 | async-start | bytes 2048000 | tf_op jit(solution)/shard_map/psum | solution.py:32
  128.5 1.6 copy-start.2
  128.5 2.3 copy-start.3
  136.9 34.2 %all-to-all-start.1 = ((bf16[8,16,16,1,136]{4,1,0,3,2:T(8,128)(2,1)}), bf16[8,16,16,1,136]{4,1,0,3,2:T(8,128)(2,1)S(1)}, u32[]{:S(2)}, u32[]{:S(2)}) async-start(bf16[8,16,16,1,136]{4,1,0,3,2:T(8,128)(2,1)} %copy.25), calls=%async_computation.2 | async-start | bytes 2097152 | tf_op jit(solution)/shard_map/all_to_all | solution.py:28
  144.0 50.3 %all-reduce.5.cloned.1.call-start = ((), (), s32[]{:S(2)}) async-start(), calls=%async_computation.6 | async-start | bytes 1048576 | tf_op jit(solution)/shard_map/psum | solution.py:34
  148.9 98.8 %all-gather.2.cloned.1.call-start = ((), (), s32[]{:S(2)}) async-start(), calls=%async_computation.4 | async-start | bytes 5242880 | tf_op jit(solution)/shard_map/all_gather | solution.py:29
  194.3 6.9 %copy-start.1 = (f32[8,16,16,1,136]{4,1,2,0,3:T(8,128)S(1)}, f32[8,16,16,1,136]{4,1,2,0,3:T(8,128)}, u32[]{:S(2)}) copy-start(f32[8,16,16,1,136]{4,1,2,0,3:T(8,128)} %get-tuple-element.22) | copy-start | bytes 3342340
Sparse Core Ops, SparseCore 0:
  14.1 53.1 reduce-scatter.1
  82.4 50.1 all-reduce.2
  149.0 45.2 all-reduce.4
  196.6 51.0 all-gather.1
where the time goes:
time: 261 us; the launch traced here: 260 us
  waiting for transfers between devices  186 us (71%)
  local copies, waits for them, and re-layouts  23.8 us (9%)
  starting transfers between devices  16.7 us (6%)
  between operations  13.8 us (5%)
  matrix products  11.7 us (4%)
  other arithmetic  8.55 us (3%)
    reduce_scatter x1, waiting for transfers between devices, per_device(): lax.psum_scatter(local_weights.astype(jnp.float32).astype(jnp.bfloat16),...  53.3 us
    all_to_all x1, waiting for transfers between devices, per_device(): lax.all_to_all(part, 'shard', split_axis=1, concat_axis=2, tiled=True)  48.4 us
    all_gather x1, waiting for transfers between devices, per_device(): whole = lax.all_gather(columns, 'group', axis=1, tiled=True)  39 us
    psum x1, waiting for transfers between devices, per_device(): lax.psum(jnp.dot(difference, basis, precision=lax.Precision.HIGHEST), 'te...  22.1 us
    all_to_all x1, waiting for transfers between devices, per_device(): lax.all_to_all(stepped_half, 'shard', split_axis=2, concat_axis=1, tiled=...  21.9 us
    unnamed x12, local copies, waits for them, and re-layouts  21.6 us
    all_to_all x1, starting transfers between devices, per_device(): lax.all_to_all(part, 'shard', split_axis=1, concat_axis=2, tiled=True)  9.24 us
    all_to_all x1, starting transfers between devices, per_device(): lax.all_to_all(stepped_half, 'shard', split_axis=2, concat_axis=1, tiled=...  7.1 us
  transfers between devices with their start and end apart: 6, of which 5 were waited for; matrix products, arithmetic and copies ran while one was open for 10% of the time, Pallas kernels for 0%

commit v1 on v0

--- a/solution.py
+++ b/solution.py
@@ -25,7 +25,15 @@
     moved = momentum_decay * momentum + delta
     stepped = anchor - outer_rate * (delta + momentum_decay * moved)
     stepped_half = stepped.astype(jnp.bfloat16)
-    columns = lax.all_to_all(stepped_half, "shard", split_axis=2, concat_axis=1, tiled=True)
+
+    def launch_object(mat):
+        state_now = lax.axis_size("shard")
+        t_next = jnp.split(mat, state_now, 2)
+        state_next = jnp.stack(t_next, axis=0)
+        current_arr = lax.all_to_all(state_next, axis_name="shard", split_axis=0, concat_axis=0)
+        return jnp.concatenate(current_arr, 1)
+
+    columns = launch_object(stepped_half)
     whole = lax.all_gather(columns, "group", axis=1, tiled=True)
     new_weights = whole.reshape(layers, width, block)
     local_embedding = group_embedding[0].astype(jnp.float32)

time: 261 us -> 270 us (1.034)
  local copies, waits for them, and re-layouts: 23.8 us -> 32.8 us
    unnamed x12 -> x27, local copies, waits for them, and re-layouts: 21.6 us -> 31.1 us
  transfers between devices with their start and end apart: 6 -> 6, of which waited for: 5 -> 5; matrix products, arithmetic and copies ran while one was open for 10% -> 13% of each run, Pallas kernels for 0% -> 0%
where the time goes in v1:
time: 270 us; the launch traced here: 269 us
  waiting for transfers between devices  186 us (69%)
  local copies, waits for them, and re-layouts  32.8 us (12%)
  starting transfers between devices  16.7 us (6%)
  between operations  13.8 us (5%)
  matrix products  11.7 us (4%)
  other arithmetic  8.55 us (3%)
    reduce_scatter x1, waiting for transfers between devices, per_device(): lax.psum_scatter(local_weights.astype(jnp.float32).astype(jnp.bfloat16),...  53.3 us
    all_to_all x1, waiting for transfers between devices, per_device(): lax.all_to_all(part, 'shard', split_axis=1, concat_axis=2, tiled=True)  48.4 us
    all_gather x1, waiting for transfers between devices, per_device(): whole = lax.all_gather(columns, 'group', axis=1, tiled=True)  39 us
    unnamed x27, local copies, waits for them, and re-layouts  31.1 us
    psum x1, waiting for transfers between devices, per_device(): lax.psum(jnp.dot(difference, basis, precision=lax.Precision.HIGHEST), 'te...  22.1 us
    all_to_all x1, waiting for transfers between devices, launch_object(): lax.all_to_all(state_next, axis_name='shard', split_axis=0, concat_axis=0)  21.9 us
    all_to_all x1, starting transfers between devices, per_device(): lax.all_to_all(part, 'shard', split_axis=1, concat_axis=2, tiled=True)  9.24 us
    all_to_all x1, starting transfers between devices, launch_object(): lax.all_to_all(state_next, axis_name='shard', split_axis=0, concat_axis=0)  7.1 us
  transfers between devices with their start and end apart: 6, of which 5 were waited for; matrix products, arithmetic and copies ran while one was open for 13% of the time, Pallas kernels for 0%

profile of v1, /device:TPU:1, one launch (start us, length us, event | category | flops | bytes accessed | tf_op | source)
XLA Modules:
  0.0 269.2 jit_solution(12529051423488278)
XLA Ops:
  7.2 6.8 %copy.51 = bf16[1,8,1024,136]{3,1,2,0:T(8,128)(2,1)} copy(bf16[1,8,1024,136]{2,3,1,0:T(8,128)(2,1)} %param.7) | data formatting | bytes 4456448 | tf_op args[0]
  14.0 53.3 %reduce-scatter.2.cloned.1.call-done = bf16[8,256,136]{2,0,1:T(8,128)(2,1)} async-done(((bf16[8,1024,136]{2,0,1:T(8,128)(2,1)}), bf16[8,256,136]{2,0,1:T(8,128)(2,1)}) %reduce-scatter.2.cloned.1.call-update) | async-done | bytes 557072 | tf_op jit(solution)/shard_map/reduce_scatter | solution.py:16
  67.3 2.7 %bitcast_convert_fusion = f32[8,256,1,1,136]{4,0,3,2,1:T(8,128)} fusion(bf16[8,256,136]{2,0,1:T(8,128)(2,1)} %reduce-scatter.2.cloned.1.call-done), kind=kLoop, calls=%fused_computation.11 | loop fusion | flops 278528 | bytes 1671168 | tf_op jit(solution)/shard_map/reshape | solution.py:22
  70.0 9.2 %all-to-all-start = ((f32[8,256,1,1,136]{4,0,3,2,1:T(8,128)}), f32[8,256,1,1,136]{4,0,3,2,1:T(8,128)S(1)}, u32[]{:S(2)}, u32[]{:S(2)}) async-start(f32[8,256,1,1,136]{4,0,3,2,1:T(8,128)} %bitcast_convert_fusion), calls=%async_computation.1 | async-start | bytes 4194304 | tf_op jit(solution)/shard_map/all_to_all | solution.py:23
  79.3 0.7 all-reduce.3.cloned.1.call-update
  80.0 48.4 %all-to-all-done = f32[8,256,1,1,136]{4,0,3,2,1:T(8,128)S(1)} async-done(((f32[8,256,1,1,136]{4,0,3,2,1:T(8,128)}), f32[8,256,1,1,136]{4,0,3,2,1:T(8,128)S(1)}, u32[]{:S(2)}, u32[]{:S(2)}) %all-to-all-start) | async-done | bytes 1114144 | tf_op jit(solution)/shard_map/all_to_all | solution.py:23
  128.5 0.7 copy_multiply_fusion.1
  129.2 0.9 copy-done.2
  130.1 0.6 copy-done.3
  130.7 5.1 %fusion.24 = (bf16[8,16,16,1,136]{4,1,2,0,3:T(8,128)(2,1)S(1)}, f32[8,16,16,1,136]{4,1,2,0,3:T(8,128)}, f32[8,16,16,1,136]{4,1,2,0,3:T(8,128)S(1)}) fusion(f32[8,16,16,1,136]{4,3,2,1,0:T(1,128)S(1)} %copy-done.2, f32[8,16,16,1,136]{4,1,2,0,3:T(8,128)S(1)} %bitcast.111, f32[8,16,16,1,136]{4,3,2,1,0:T(1,128)S(1)} %copy-done.3), kind=kLoop, calls=%fused_computation.47 | loop fusion | flops 2228224 | bytes 6127616 | tf_op jit(solution)/shard_map/convert_element_type | solution.py:27
  135.8 0.6 fusion.21
  136.5 0.6 fusion.20
  137.1 0.6 fusion.19
  137.7 0.6 fusion.18
  138.4 0.6 fusion.17
  139.0 0.6 fusion.16
  139.6 0.6 fusion.15
  140.3 0.6 fusion.14
  140.9 0.6 fusion.13
  141.5 0.6 fusion.12
  142.2 0.6 fusion.11
  142.8 0.6 fusion.10
  146.0 7.1 %all-to-all-start.1 = ((bf16[16,8,16,1,1,136]{5,2,1,4,3,0:T(8,128)(2,1)}), bf16[16,8,16,1,1,136]{5,2,1,4,3,0:T(8,128)(2,1)S(1)}, u32[]{:S(2)}, u32[]{:S(2)}) async-start(bf16[16,8,16,1,1,136]{5,2,1,4,3,0:T(8,128)(2,1)} %fusion.6), calls=%async_computation.2 | async-start | bytes 2097152 | tf_op jit(solution)/shard_map/all_to_all | solution.py:33
  153.2 4.8 %fusion.1 = f32[2000,64]{0,1:T(8,128)} fusion(f32[256,64]{0,1:T(8,128)S(1)} %copy-done, f32[2000,256]{1,0:T(8,128)} %param.11, bf16[2000,256]{1,0:T(8,128)(2,1)} %all-reduce.3.cloned.1.call-done), kind=kOutput, calls=%fused_computation.6 | convolution fusion | flops 394752000 | bytes 3649536 | tf_op jit(solution)/shard_map/dot_general | solution.py:42
  158.2 21.9 %all-to-all-done.1 = bf16[16,8,16,1,1,136]{5,2,1,4,3,0:T(8,128)(2,1)S(1)} async-done(((bf16[16,8,16,1,1,136]{5,2,1,4,3,0:T(8,128)(2,1)}), bf16[16,8,16,1,1,136]{5,2,1,4,3,0:T(8,128)(2,1)S(1)}, u32[]{:S(2)}, u32[]{:S(2)}) %all-to-all-start.1) | async-done | bytes 557088 | tf_op jit(solution)/shard_map/all_to_all | solution.py:33
  180.1 1.1 copy.71
  181.2 22.1 %all-reduce.5.cloned.1.call-done = f32[2000,64]{0,1:T(8,128)} async-done(((f32[2000,64]{0,1:T(8,128)}), f32[2000,64]{0,1:T(8,128)}) %all-reduce.5.cloned.1.call-update) | async-done | bytes 512016 | tf_op jit(solution)/shard_map/psum | solution.py:42
  203.4 6.9 %fusion.23 = (bf16[2000,256]{1,0:T(8,128)(2,1)}, f32[2000,256]{1,0:T(8,128)}, f32[2000,256]{1,0:T(8,128)}) fusion(f32[2000,256]{1,0:T(8,128)} %param.11, f32[2000,256]{1,0:T(8,128)} %param.12, f32[2000,64]{0,1:T(8,128)} %all-reduce.5.cloned.1.call-done, f32[256,64]{0,1:T(8,128)S(1)} %copy-done), kind=kOutput, calls=%fused_computation.46 | convolution fusion | flops 396800000 | bytes 9793536 | tf_op jit(solution)/shard_map/dot_general | solution.py:43
  210.3 3.7 %copy.73 = f32[8,16,16,1,136]{4,3,2,1,0:T(1,128)} copy(f32[8,16,16,1,136]{4,1,2,0,3:T(8,128)S(1)} %copy-done.1) | data formatting | bytes 2228224
  214.0 3.7 %copy.74 = f32[8,16,16,1,136]{4,3,2,1,0:T(1,128)} copy(f32[8,16,16,1,136]{4,1,2,0,3:T(8,128)S(1)} %get-tuple-element.23) | data formatting | bytes 2228224
  217.8 39.0 %all-gather.2.cloned.1.call-done = bf16[8,1024,1,1,136]{4,1,0,3,2:T(8,128)(2,1)} async-done(((bf16[8,256,1,1,136]{4,1,0,3,2:T(8,128)(2,1)}), bf16[8,1024,1,1,136]{4,1,0,3,2:T(8,128)(2,1)}) %all-gather.2.cloned.1.call-update) | async-done | bytes 2228240 | tf_op jit(solution)/shard_map/all_gather | solution.py:37
  256.7 5.9 %copy.72 = bf16[8,1024,136]{1,2,0:T(8,128)(2,1)} copy(bf16[8,1024,136]{2,1,0:T(8,128)(2,1)} %bitcast.112) | data formatting | bytes 4456448
  (18 shorter events, 3.0 us)
Async XLA Ops:
  7.2 146.0 %copy-start = (f32[256,64]{0,1:T(8,128)S(1)}, f32[256,64]{0,1:T(8,128)}, u32[]{:S(2)}) copy-start(f32[256,64]{0,1:T(8,128)} %param.13) | copy-start | bytes 196612
  7.2 60.1 %reduce-scatter.2.cloned.1.call-start = ((), (), s32[]{:S(2)}) async-start(), calls=%async_computation.3 | async-start | bytes 5242880 | tf_op jit(solution)/shard_map/reduce_scatter | solution.py:16
  70.0 58.4 %all-to-all-start = ((f32[8,256,1,1,136]{4,0,3,2,1:T(8,128)}), f32[8,256,1,1,136]{4,0,3,2,1:T(8,128)S(1)}, u32[]{:S(2)}, u32[]{:S(2)}) async-start(f32[8,256,1,1,136]{4,0,3,2,1:T(8,128)} %bitcast_convert_fusion), calls=%async_computation.1 | async-start | bytes 4194304 | tf_op jit(solution)/shard_map/all_to_all | solution.py:23
  79.3 73.9 %all-reduce.3.cloned.1.call-start = ((), (), s32[]{:S(2)}) async-start(), calls=%async_computation.5 | async-start | bytes 2048000 | tf_op jit(solution)/shard_map/psum | solution.py:40
  128.5 1.6 copy-start.2
  128.5 2.3 copy-start.3
  146.0 34.2 %all-to-all-start.1 = ((bf16[16,8,16,1,1,136]{5,2,1,4,3,0:T(8,128)(2,1)}), bf16[16,8,16,1,1,136]{5,2,1,4,3,0:T(8,128)(2,1)S(1)}, u32[]{:S(2)}, u32[]{:S(2)}) async-start(bf16[16,8,16,1,1,136]{5,2,1,4,3,0:T(8,128)(2,1)} %fusion.6), calls=%async_computation.2 | async-start | bytes 2097152 | tf_op jit(solution)/shard_map/all_to_all | solution.py:33
  153.1 50.3 %all-reduce.5.cloned.1.call-start = ((), (), s32[]{:S(2)}) async-start(), calls=%async_computation.6 | async-start | bytes 1048576 | tf_op jit(solution)/shard_map/psum | solution.py:42
  158.0 98.8 %all-gather.2.cloned.1.call-start = ((), (), s32[]{:S(2)}) async-start(), calls=%async_computation.4 | async-start | bytes 5242880 | tf_op jit(solution)/shard_map/all_gather | solution.py:37
  203.4 6.9 %copy-start.1 = (f32[8,16,16,1,136]{4,1,2,0,3:T(8,128)S(1)}, f32[8,16,16,1,136]{4,1,2,0,3:T(8,128)}, u32[]{:S(2)}) copy-start(f32[8,16,16,1,136]{4,1,2,0,3:T(8,128)} %get-tuple-element.22) | copy-start | bytes 3342340
Sparse Core Ops, SparseCore 0:
  14.1 53.1 reduce-scatter.1
  82.4 50.1 all-reduce.2
  158.1 45.2 all-reduce.4
  205.6 51.0 all-gather.1
